TPU v7x, 256 devices: a whole 4x4x8 slice. The times are simulated.
256 devices in a mesh: prow: 8 (over z_hi, core), pcol: 32 (over x, z_lo, y).
Axes of the slice: x: 4, y: 4, z: 8 (z_hi: 4, z_lo: 2; z = z_hi * 2 + z_lo), core: 2. Of those that a mesh axis runs over, the one named last changes fastest.
Arguments:
- slab: float32 [2048, 98304], P('pcol', 'prow'), may hold values from -6 to 6
- vectors: float32 [98304, 512], P(('prow', 'pcol')), may hold values from -0.01953125 to 0.01953125
- tfactors: float32 [4, 128, 128], replicated, as said below
Outputs:
- transformed: float32 [2048, 98304], P('pcol', 'prow')
Inputs may be any that keep to these rules, and one draw needn't show every extreme that they name: Each tfactors[k] is upper triangular with diagonal entries between 1 and 2.
All inputs are finite; a program needn't handle non-finite values.
Results may differ from a plain program's by a relative error of at most 0.0001.
Values sent between devices are 32-bit elements; how exact they have to be, the bound alone decides.
No kernel may reach another device: no remote copies, remote signals or barrier semaphores. Data moves between devices by JAX's collectives and lax.ppermute only.
A program may use at most 128 MiB of HBM per device.

v0:
```python
import jax
import jax.numpy as jnp
from jax import lax
from jax.sharding import Mesh
from jax.sharding import PartitionSpec as P

PCOL_PARTS = (4, 2, 4)
GROUP = ("zl", "y")


def matmul(left, right):
    return jnp.dot(left, right, precision=lax.Precision.HIGHEST, preferred_element_type=jnp.float32)


def per_device(slab, vectors, tfactors):
    rows, cols = slab.shape
    depth = vectors.shape[0]
    count = tfactors.shape[0]
    width = tfactors.shape[1]
    nx = PCOL_PARTS[0]
    ng = PCOL_PARTS[1] * PCOL_PARTS[2]
    gram = lax.psum(
        matmul(vectors[:, width:].T, vectors[:, : (count - 1) * width]), ("prow", "x", "zl", "y")
    )
    basis = lax.all_gather(vectors, "x", axis=0, tiled=True)
    work = slab.reshape(rows, nx, ng, depth).transpose(2, 0, 1, 3)
    work = lax.all_to_all(work, GROUP, 0, 0, tiled=True).reshape(ng * rows, nx * depth)
    products = lax.psum(matmul(work, basis), ("zl", "y", "prow"))
    scaled = [None] * count
    for k in reversed(range(count)):
        part = products[:, k * width : (k + 1) * width]
        for j in range(k + 1, count):
            block = gram[(j - 1) * width : j * width, k * width : (k + 1) * width]
            part = part - matmul(scaled[j], block)
        scaled[k] = matmul(part, tfactors[k].T)
    scaled = jnp.concatenate(scaled, axis=1)
    work = work - matmul(scaled, basis.T)
    work = work.reshape(ng, rows, nx, depth)
    work = lax.all_to_all(work, GROUP, 0, 0, tiled=True)
    return work.transpose(1, 2, 0, 3).reshape(rows, cols)


def solution(mesh):
    devices = mesh.devices.reshape((mesh.shape["prow"],) + PCOL_PARTS)
    fine = Mesh(devices, ("prow", "x", "zl", "y"))
    cols = ("x", "zl", "y")
    in_specs = (P(cols, "prow"), P(("prow",) + cols, None), P())
    out_specs = P(cols, "prow")
    return jax.shard_map(
        per_device, mesh=fine, in_specs=in_specs, out_specs=out_specs, check_vma=False
    )
```

profile of v0, /device:TPU:2, one launch (start us, length us, event | category | flops | bytes accessed | tf_op | source)
XLA Modules:
  0.0 592.0 jit_solution(9328307342298171551)
XLA Ops:
  6.5 2.4 copy.6
  9.0 2.5 copy.10
  11.5 5.8 all-to-all-start
  18.1 36.5 %all-to-all-done = f32[8,64,4,384]{3,2,1,0:T(4,128)S(1)} async-done(((f32[8,64,4,384]{3,2,1,0:T(4,128)}), f32[8,64,4,384]{3,2,1,0:T(4,128)S(1)}, u32[]{:S(2)}, u32[]{:S(2)}) %all-to-all-start) | async-done | bytes 3145760 | tf_op jit(solution)/shard_map/all_to_all | solution.py:27
  54.6 1.7 copy-done.1
  56.2 2.1 copy.7
  58.3 5.3 all-gather.2.cloned.1.call-done
  63.6 7.5 %fusion.30 = f32[512,512]{1,0:T(8,128)} fusion(f32[512,1536]{1,0:T(8,128)S(1)} %bitcast.37, f32[1536,512]{1,0:T(8,128)} %all-gather.2.cloned.1.call-done), kind=kOutput, calls=%fused_computation.38 | convolution fusion | flops 4831838208 | bytes 7340032 | tf_op jit(solution)/shard_map/dot_general | solution.py:12
  71.3 3.4 fusion.7
  74.8 182.7 %all-reduce.3.cloned.1.call-done = f32[512,512]{1,0:T(8,128)} async-done(((f32[512,512]{1,0:T(8,128)}), f32[512,512]{1,0:T(8,128)}) %all-reduce.3.cloned.1.call-update) | async-done | bytes 1048592 | tf_op jit(solution)/shard_map/psum | solution.py:28
  257.4 1.3 fusion.10
  258.8 252.0 %all-reduce.5.cloned.1.call-done = f32[384,384]{1,0:T(8,128)} async-done(((f32[384,384]{1,0:T(8,128)}), f32[384,384]{1,0:T(8,128)}) %all-reduce.5.cloned.1.call-update) | async-done | bytes 589840 | tf_op jit(solution)/shard_map/psum | solution.py:22
  510.8 1.6 convolution_subtract_fusion.6
  512.4 1.4 fusion.22
  513.8 1.6 convolution_subtract_fusion.5
  515.4 1.4 convolution_subtract_fusion.4
  517.2 1.6 convolution_subtract_fusion.3
  518.8 1.4 convolution_subtract_fusion.2
  520.3 1.4 convolution_subtract_fusion.1
  522.1 12.2 %convolution_subtract_fusion = f32[512,1536]{1,0:T(8,128)} fusion(f32[512,1536]{1,0:T(8,128)S(1)} %bitcast.38, f32[1536,512]{1,0:T(8,128)S(1)} %copy-done, f32[512,128]{0,1:T(8,128)S(1)} %fusion.10, f32[512,128]{0,1:T(8,128)S(1)} %fusion.22, f32[512,128]{0,1:T(8,128)S(1)} %fusion.20, f32[512,128]{0,1:T(8,128)S(1)} %fusion.18), kind=kOutput, calls=%fused_computation | convolution fusion | flops 4833411072 | bytes 10485760 | tf_op jit(solution)/shard_map/dot_general | solution.py:12
  534.3 3.2 reshape.14
  537.5 42.7 %all_to_all.10 = f32[8,64,4,384]{3,2,1,0:T(4,128)S(1)} all-to-all(f32[8,64,4,384]{3,2,1,0:T(4,128)S(1)} %reshape.14), channel_id=1, replica_groups=mesh['prow'=8,'x'=4,'zl'=2,'y'=4] {'zl','y'}, dimensions={0} | all-to-all | bytes 6291456 | tf_op jit(solution)/shard_map/all_to_all | solution.py:39
  580.2 1.8 copy.5
  582.0 3.4 copy.8
  (13 shorter events, 1.8 us)
Async XLA Ops:
  11.5 43.1 %all-to-all-start = ((f32[8,64,4,384]{3,2,1,0:T(4,128)}), f32[8,64,4,384]{3,2,1,0:T(4,128)S(1)}, u32[]{:S(2)}, u32[]{:S(2)}) async-start(f32[8,64,4,384]{3,2,1,0:T(4,128)} %bitcast.40), calls=%async_computation | async-start | bytes 6291456 | tf_op jit(solution)/shard_map/all_to_all | solution.py:27
  17.3 46.3 %all-gather.2.cloned.1.call-start = ((), (), s32[]{:S(2)}) async-start(), calls=%async_computation.2 | async-start | bytes 3932160 | tf_op jit(solution)/shard_map/all_gather | solution.py:25
  18.0 239.4 %all-reduce.3.cloned.1.call-start = ((), (), s32[]{:S(2)}) async-start(), calls=%async_computation.3 | async-start | bytes 2097152 | tf_op jit(solution)/shard_map/psum | solution.py:28
  54.6 1.7 copy-start.1
  71.1 439.6 %all-reduce.5.cloned.1.call-start = ((), (), s32[]{:S(2)}) async-start(), calls=%async_computation.4 | async-start | bytes 1179648 | tf_op jit(solution)/shard_map/psum | solution.py:22
  510.8 6.1 %copy-start.2 = (f32[4,128,128]{2,1,0:T(8,128)S(1)}, f32[4,128,128]{2,1,0:T(8,128)}, u32[]{:S(2)}) copy-start(f32[4,128,128]{2,1,0:T(8,128)} %param.5) | copy-start | bytes 786436
  512.4 9.7 %copy-start = (f32[1536,512]{1,0:T(8,128)S(1)}, f32[1536,512]{1,0:T(8,128)}, u32[]{:S(2)}) copy-start(f32[1536,512]{1,0:T(8,128)} %all-gather.2.cloned.1.call-done) | copy-start | bytes 9437188
Sparse Core Ops, SparseCore 0:
  19.9 43.6 all-gather.1
  71.2 186.1 all-reduce.2
  263.9 246.8 all-reduce.4
where the time goes:
time: 593 us; the launch traced here: 592 us
  waiting for transfers between devices  477 us (80%)
  blocking collectives  42.7 us (7%)
  matrix products  35.6 us (6%)
  local copies, waits for them, and re-layouts  17.1 us (3%)
  between operations  13.2 us (2%)
  starting transfers between devices  6.12 us (1%)
    psum x1, waiting for transfers between devices, per_device(): lax.psum(matmul(vectors[:, width:].T, vectors[:, :(count - 1) * width]),...  252 us
    psum x1, waiting for transfers between devices, per_device(): products = lax.psum(matmul(work, basis), ('zl', 'y', 'prow'))  183 us
    all_to_all x1, blocking collectives, per_device(): work = lax.all_to_all(work, GROUP, 0, 0, tiled=True)  42.7 us
    all_to_all x1, waiting for transfers between devices, per_device(): lax.all_to_all(work, GROUP, 0, 0, tiled=True).reshape(ng * rows, nx * depth)  36.5 us
    dot_general x13, matrix products, matmul(): jnp.dot(left, right, precision=lax.Precision.HIGHEST, preferred_element_t...  35.6 us
  transfers between devices with their start and end apart: 4, of which 4 were waited for; matrix products, arithmetic and copies ran while one was open for 1% of the time, Pallas kernels for 0%

commit v1 on v0

--- a/solution.py
+++ b/solution.py
@@ -25,7 +25,7 @@
     basis = lax.all_gather(vectors, "x", axis=0, tiled=True)
     work = slab.reshape(rows, nx, ng, depth).transpose(2, 0, 1, 3)
     work = lax.all_to_all(work, GROUP, 0, 0, tiled=True).reshape(ng * rows, nx * depth)
-    products = lax.psum(matmul(work, basis), ("zl", "y", "prow"))
+    products = jnp.sum(lax.all_gather(matmul(work, basis), ("zl", "y", "prow")), axis=0)
     scaled = [None] * count
     for k in reversed(range(count)):
         part = products[:, k * width : (k + 1) * width]

time: 593 us -> 648 us (1.093)
  waiting for transfers between devices: 477 us -> 509 us
  other arithmetic: 0 us -> 22.1 us
    all_gather x0 -> x1, waiting for transfers between devices: none -> 365 us  [per_device(): lax.all_gather(matmul(work, basis), ('zl', 'y', 'prow'))]
    psum x1 -> x0, waiting for transfers between devices: 183 us -> none  [per_device(): products = lax.psum(matmul(work, basis), ('zl', 'y', 'prow'))]
    psum x1, waiting for transfers between devices: 252 us -> 102 us  [per_device(): lax.psum(matmul(vectors[:, width:].T, vectors[:, :(count - 1) * width]),...]
    reduce_sum x0 -> x1, other arithmetic: none -> 22.1 us  [per_device(): jnp.sum(lax.all_gather(matmul(work, basis), ('zl', 'y', 'prow')), axis=0)]
  transfers between devices with their start and end apart: 4 -> 4, of which waited for: 4 -> 4; matrix products, arithmetic and copies ran while one was open for 1% -> 4% of each run, Pallas kernels for 0% -> 0%
where the time goes in v1:
time: 648 us
  waiting for transfers between devices  509 us (79%)
  blocking collectives  42.8 us (7%)
  matrix products  35.6 us (5%)
  other arithmetic  22.1 us (3%)
  local copies, waits for them, and re-layouts  17.1 us (3%)
  between operations  15 us (2%)
    all_gather x1, waiting for transfers between devices, per_device(): lax.all_gather(matmul(work, basis), ('zl', 'y', 'prow'))  365 us
    psum x1, waiting for transfers between devices, per_device(): lax.psum(matmul(vectors[:, width:].T, vectors[:, :(count - 1) * width]),...  102 us
    all_to_all x1, blocking collectives, per_device(): work = lax.all_to_all(work, GROUP, 0, 0, tiled=True)  42.8 us
    all_to_all x1, waiting for transfers between devices, per_device(): lax.all_to_all(work, GROUP, 0, 0, tiled=True).reshape(ng * rows, nx * depth)  36.5 us
    dot_general x13, matrix products, matmul(): jnp.dot(left, right, precision=lax.Precision.HIGHEST, preferred_element_t...  35.6 us
    reduce_sum x1, other arithmetic, per_device(): jnp.sum(lax.all_gather(matmul(work, basis), ('zl', 'y', 'prow')), axis=0)  22.1 us
  transfers between devices with their start and end apart: 4, of which 4 were waited for; matrix products, arithmetic and copies ran while one was open for 4% of the time, Pallas kernels for 0%

profile of v1, /device:TPU:2, one launch (start us, length us, event | category | flops | bytes accessed | tf_op | source)
XLA Modules:
  0.0 647.5 jit_solution(15395744205558190033)
XLA Ops:
  7.4 2.4 copy.6
  9.8 2.5 copy.10
  12.3 5.8 all-to-all-start
  18.9 36.5 %all-to-all-done = f32[8,64,4,384]{3,2,1,0:T(4,128)S(1)} async-done(((f32[8,64,4,384]{3,2,1,0:T(4,128)}), f32[8,64,4,384]{3,2,1,0:T(4,128)S(1)}, u32[]{:S(2)}, u32[]{:S(2)}) %all-to-all-start) | async-done | bytes 3145760 | tf_op jit(solution)/shard_map/all_to_all | solution.py:27
  55.4 1.7 copy-done.1
  57.1 2.1 copy.7
  59.2 5.3 all-gather.4.cloned.1.call-done
  64.5 7.5 %fusion.30 = f32[512,512]{1,0:T(8,128)} fusion(f32[512,1536]{1,0:T(8,128)S(1)} %bitcast.38, f32[1536,512]{1,0:T(8,128)} %all-gather.4.cloned.1.call-done), kind=kOutput, calls=%fused_computation.38 | convolution fusion | flops 4831838208 | bytes 7340032 | tf_op jit(solution)/shard_map/dot_general | solution.py:12
  72.0 3.4 fusion.7
  75.4 364.8 %all-gather.6.cloned.1.call-done = f32[32768,512]{1,0:T(8,128)} async-done(((f32[512,512]{1,0:T(8,128)}), f32[32768,512]{1,0:T(8,128)}) %all-gather.6.cloned.1.call-update) | async-done | bytes 67108880 | tf_op jit(solution)/shard_map/all_gather | solution.py:28
  440.2 22.1 %reduce_sum.9 = f32[512,512]{1,0:T(8,128)} reduce(f32[64,512,512]{2,1,0:T(8,128)} %bitcast.1, f32[]{:T(128)} %constant.0.clone.1), dimensions={0}, to_apply=%region_0.0 | reduce | flops 16515072 | bytes 68157440 | tf_op jit(solution)/shard_map/reduce_sum | solution.py:28
  463.7 101.6 %all-reduce.2.cloned.1.call-done = f32[384,384]{1,0:T(8,128)} async-done(((f32[384,384]{1,0:T(8,128)}), f32[384,384]{1,0:T(8,128)}) %all-reduce.2.cloned.1.call-update) | async-done | bytes 589840 | tf_op jit(solution)/shard_map/psum | solution.py:22
  565.3 1.6 convolution_subtract_fusion.6
  566.9 1.4 fusion.22
  568.3 1.6 convolution_subtract_fusion.5
  569.9 1.4 convolution_subtract_fusion.4
  571.7 1.6 convolution_subtract_fusion.3
  573.3 1.4 convolution_subtract_fusion.2
  574.8 1.4 convolution_subtract_fusion.1
  576.6 12.2 %convolution_subtract_fusion = f32[512,1536]{1,0:T(8,128)} fusion(f32[512,1536]{1,0:T(8,128)S(1)} %bitcast.39, f32[1536,512]{1,0:T(8,128)S(1)} %copy-done, f32[512,128]{0,1:T(8,128)S(1)} %fusion.10, f32[512,128]{0,1:T(8,128)S(1)} %fusion.22, f32[512,128]{0,1:T(8,128)S(1)} %fusion.20, f32[512,128]{0,1:T(8,128)S(1)} %fusion.18), kind=kOutput, calls=%fused_computation | convolution fusion | flops 4833411072 | bytes 10485760 | tf_op jit(solution)/shard_map/dot_general | solution.py:12
  588.8 3.2 reshape.14
  592.0 42.8 %all_to_all.10 = f32[8,64,4,384]{3,2,1,0:T(4,128)S(1)} all-to-all(f32[8,64,4,384]{3,2,1,0:T(4,128)S(1)} %reshape.14), channel_id=1, replica_groups=mesh['prow'=8,'x'=4,'zl'=2,'y'=4] {'zl','y'}, dimensions={0} | all-to-all | bytes 6291456 | tf_op jit(solution)/shard_map/all_to_all | solution.py:39
  634.8 1.8 copy.5
  636.6 3.4 copy.8
  (14 shorter events, 3.0 us)
Async XLA Ops:
  12.3 43.1 %all-to-all-start = ((f32[8,64,4,384]{3,2,1,0:T(4,128)}), f32[8,64,4,384]{3,2,1,0:T(4,128)S(1)}, u32[]{:S(2)}, u32[]{:S(2)}) async-start(f32[8,64,4,384]{3,2,1,0:T(4,128)} %bitcast.41), calls=%async_computation | async-start | bytes 6291456 | tf_op jit(solution)/shard_map/all_to_all | solution.py:27
  18.1 46.3 %all-gather.4.cloned.1.call-start = ((), (), s32[]{:S(2)}) async-start(), calls=%async_computation.2 | async-start | bytes 3932160 | tf_op jit(solution)/shard_map/all_gather | solution.py:25
  18.8 421.4 %all-gather.6.cloned.1.call-start = ((), (), s32[]{:S(2)}) async-start(), calls=%async_computation.4 | async-start | bytes 68157440 | tf_op jit(solution)/shard_map/all_gather | solution.py:28
  55.4 1.7 copy-start.1
  72.0 493.3 %all-reduce.2.cloned.1.call-start = ((), (), s32[]{:S(2)}) async-start(), calls=%async_computation.3 | async-start | bytes 1179648 | tf_op jit(solution)/shard_map/psum | solution.py:22
  565.3 6.1 copy-start.2
  566.9 9.7 %copy-start = (f32[1536,512]{1,0:T(8,128)S(1)}, f32[1536,512]{1,0:T(8,128)}, u32[]{:S(2)}) copy-start(f32[1536,512]{1,0:T(8,128)} %all-gather.4.cloned.1.call-done) | copy-start | bytes 9437188
Sparse Core Ops, SparseCore 0:
  20.8 43.6 all-gather.3
  72.1 368.1 all-gather.5
Sparse Core Ops, SparseCore 1:
  77.9 487.3 all-reduce.1
